TPU v7x, 512 devices: a whole 4x4x16 slice. The times are simulated.
512 devices in a mesh: patch: 128 (over z, y, core), mp: 4 (over x).
Axes of the slice: x: 4, y: 4, z: 16, core: 2. Of those that a mesh axis runs over, the one named last changes fastest.
Arguments:
- features: bfloat16 [65536, 1024], P('patch'), may hold values from -16 to 16
- gain_attn: float32 [1024], replicated, may hold values from 0.1 to 1.9
- w_qkv: bfloat16 [3, 1024, 1024], P(None, None, 'mp'), as said below
- w_out: bfloat16 [1024, 1024], P('mp'), may hold values from -0.1875 to 0.1875
- gain_mlp: float32 [1024], replicated, may hold values from 0.1 to 1.9
- w_up: bfloat16 [1024, 2048], P(None, 'mp'), may hold values from -0.1875 to 0.1875
- w_down: bfloat16 [2048, 1024], P('mp'), may hold values from -0.125 to 0.125
- neighbours: int32 [512, 8], replicated, may hold values from 0 to 511, as said below
Outputs:
- layer_out: bfloat16 [65536, 1024], P('patch', 'mp')
Inputs may be any that keep to these rules, and one draw needn't show every extreme that they name: `neighbours`: row p lists 8 different patches; the first is p itself. Patch q belongs to device q // 4 of the patch axis, and every listed patch belongs to a device whose index differs from that of p's device by at most 2 around the patch axis (the lining closes into a cycle). `w_qkv`: projection weights of mean zero.
All inputs are finite; a program needn't handle non-finite values.
Results may differ from a plain program's by a relative error of at most 0.012.
Values may be sent and summed in bfloat16 or wider, within the bound.
No kernel may reach another device: no remote copies, remote signals or barrier semaphores. Data moves between devices by JAX's collectives and lax.ppermute only.
A program may use at most 64 MiB of HBM per device.

v0:
```python
import jax
import jax.numpy as jnp
from jax import lax
from jax.sharding import PartitionSpec as P

D = 1024
HD = 64
PN = 128
K_NB = 8
REACH = 2


def from_behind(array, axis, by):
    length = lax.axis_size(axis)
    return lax.ppermute(array, axis, [(i, (i + by) % length) for i in range(length)])


def normalize(rows, gain):
    rows32 = rows.astype(jnp.float32)
    mean_sq = jnp.mean(rows32 * rows32, axis=-1, keepdims=True)
    return (rows32 * lax.rsqrt(mean_sq + 1e-05) * gain).astype(jnp.bfloat16)


def per_device(features, gain_attn, w_qkv, w_out, gain_mlp, w_up, w_down, neighbours):
    row_count = features.shape[0]
    patches_here = row_count // PN
    heads_here = w_qkv.shape[2] // HD
    normed = normalize(features, gain_attn)
    queries = jnp.dot(normed, w_qkv[0], preferred_element_type=jnp.float32).astype(jnp.bfloat16)
    own_keys = (
        jnp.dot(normed, w_qkv[1], preferred_element_type=jnp.float32)
        .astype(jnp.bfloat16)
        .reshape(patches_here, PN, -1)
    )
    own_vals = (
        jnp.dot(normed, w_qkv[2], preferred_element_type=jnp.float32)
        .astype(jnp.bfloat16)
        .reshape(patches_here, PN, -1)
    )
    window = {0: (own_keys, own_vals)}
    for offset in range(-REACH, REACH + 1):
        if offset != 0:
            window[offset] = from_behind((own_keys, own_vals), "patch", -offset)
    keys_win = jnp.concatenate([window[offset][0] for offset in range(-REACH, REACH + 1)], axis=0)
    vals_win = jnp.concatenate([window[offset][1] for offset in range(-REACH, REACH + 1)], axis=0)
    device = lax.axis_index("patch")
    n_dev = lax.axis_size("patch")
    listed = lax.dynamic_slice_in_dim(neighbours, device * patches_here, patches_here, 0)
    owner_dev = listed // patches_here
    offset_dev = jnp.mod(owner_dev - device + n_dev // 2, n_dev) - n_dev // 2
    slot_index = (offset_dev + REACH) * patches_here + jnp.mod(listed, patches_here)
    keys_nb = keys_win[slot_index].reshape(patches_here, K_NB * PN, heads_here, HD)
    vals_nb = vals_win[slot_index].reshape(patches_here, K_NB * PN, heads_here, HD)
    query_blk = queries.reshape(patches_here, PN, heads_here, HD)
    scores = jnp.einsum(
        "pqhd,pkhd->phqk", query_blk, keys_nb, preferred_element_type=jnp.float32
    ) * (1.0 / HD**0.5)
    probs = jax.nn.softmax(scores, axis=-1).astype(jnp.bfloat16)
    mixed_rows = jnp.einsum("phqk,pkhd->pqhd", probs, vals_nb, preferred_element_type=jnp.float32)
    attended = mixed_rows.astype(jnp.bfloat16).reshape(row_count, heads_here * HD)
    partial_value = jnp.dot(attended, w_out, preferred_element_type=jnp.float32)
    col_share = lax.psum_scatter(
        partial_value.astype(jnp.bfloat16), "mp", scatter_dimension=1, tiled=True
    ).astype(jnp.float32)
    col_width = col_share.shape[1]
    col_begin = lax.axis_index("mp") * col_width
    residual_cols = (
        lax.dynamic_slice_in_dim(features, col_begin, col_width, 1).astype(jnp.float32) + col_share
    )
    gain_cols = lax.dynamic_slice_in_dim(gain_mlp, col_begin, col_width, 0)
    square_sum = lax.psum(jnp.sum(residual_cols * residual_cols, axis=1), "mp")
    inverse_rms = lax.rsqrt(square_sum / D + 1e-05)
    normed_cols = (residual_cols * inverse_rms[:, None] * gain_cols).astype(jnp.bfloat16)
    normed2 = lax.all_gather(normed_cols, "mp", axis=1, tiled=True)
    hidden = jax.nn.gelu(
        jnp.dot(normed2, w_up, preferred_element_type=jnp.float32), approximate=True
    ).astype(jnp.bfloat16)
    down_term = jnp.dot(hidden, w_down, preferred_element_type=jnp.float32)
    down_cols = lax.psum_scatter(
        down_term.astype(jnp.bfloat16), "mp", scatter_dimension=1, tiled=True
    ).astype(jnp.float32)
    return (residual_cols + down_cols).astype(jnp.bfloat16)


def solution(mesh):
    return jax.shard_map(
        per_device,
        mesh=mesh,
        in_specs=(
            P("patch", None),
            P(),
            P(None, None, "mp"),
            P("mp", None),
            P(),
            P(None, "mp"),
            P("mp", None),
            P(),
        ),
        out_specs=P("patch", "mp"),
        check_vma=False,
    )
```

profile of v0, /device:TPU:8, one launch (start us, length us, event | category | flops | bytes accessed | tf_op | source)
XLA Modules:
  0.0 209.8 jit_solution(8594160232992480794)
XLA Ops:
  6.6 1.7 fusion.9
  8.2 1.9 convolution_convert_fusion.2
  10.1 3.5 %collective-permute-start.4 = (bf16[4,128,256]{2,1,0:T(8,128)(2,1)S(1)}, bf16[4,128,256]{2,1,0:T(8,128)(2,1)}, u32[]{:S(2)}, u32[]{:S(2)}) collective-permute-start(bf16[4,128,256]{2,1,0:T(8,128)(2,1)S(1)} %bitcast.30), channel_id=1, source_target_pairs={{0,8},{4,12},{8,16},{12,20},{16,24},{20,28},{24,32},{28,36},{32,40... | collective-permute-start | bytes 786440 | tf_op jit(solution)/shard_map/ppermute | solution.py:15
  13.6 1.9 collective-permute-start.5
  15.5 3.6 %collective-permute-start.6 = (bf16[4,128,256]{2,1,0:T(8,128)(2,1)S(1)}, bf16[4,128,256]{2,1,0:T(8,128)(2,1)S(1)}, u32[]{:S(2)}, u32[]{:S(2)}) collective-permute-start(bf16[4,128,256]{2,1,0:T(8,128)(2,1)S(1)} %bitcast.32), channel_id=1, source_target_pairs={{0,508},{4,0},{8,4},{12,8},{16,12},{20,16},{24,20},{28,24},{32,28}... | collective-permute-start | bytes 786440 | tf_op jit(solution)/shard_map/ppermute | solution.py:15
  19.2 10.4 %collective-permute-start.7 = (bf16[4,128,256]{2,1,0:T(8,128)(2,1)S(1)}, bf16[4,128,256]{2,1,0:T(8,128)(2,1)S(1)}, u32[]{:S(2)}, u32[]{:S(2)}) collective-permute-start(bf16[4,128,256]{2,1,0:T(8,128)(2,1)S(1)} %bitcast.33), channel_id=1, source_target_pairs={{0,504},{4,508},{8,0},{12,4},{16,8},{20,12},{24,16},{28,20},{32,24... | collective-permute-start | bytes 786440 | tf_op jit(solution)/shard_map/ppermute | solution.py:15
  29.7 0.5 convolution_convert_fusion.4
  30.1 1.9 collective-permute-start
  32.1 0.5 convolution_convert_fusion.3
  32.6 0.8 compare_select_fusion
  33.4 0.1 copy.17
  33.5 0.1 reshape.39
  33.5 1.0 reshape.60
  34.6 1.9 collective-permute-start.1
  36.5 1.7 constant_dynamic-update-slice_fusion.9
  38.2 3.6 %collective-permute-start.2 = (bf16[4,128,256]{2,1,0:T(8,128)(2,1)S(1)}, bf16[4,128,256]{2,1,0:T(8,128)(2,1)}, u32[]{:S(2)}, u32[]{:S(2)}) collective-permute-start(bf16[4,128,256]{2,1,0:T(8,128)(2,1)S(1)} %bitcast.27), channel_id=1, source_target_pairs={{0,508},{4,0},{8,4},{12,8},{16,12},{20,16},{24,20},{28,24},{32,28}... | collective-permute-start | bytes 786440 | tf_op jit(solution)/shard_map/ppermute | solution.py:15
  41.8 1.7 constant_dynamic-update-slice_fusion.8
  43.5 0.7 constant_dynamic-update-slice_fusion.7
  44.2 7.5 %collective-permute-start.3 = (bf16[4,128,256]{2,1,0:T(8,128)(2,1)S(1)}, bf16[4,128,256]{2,1,0:T(8,128)(2,1)}, u32[]{:S(2)}, u32[]{:S(2)}) collective-permute-start(bf16[4,128,256]{2,1,0:T(8,128)(2,1)S(1)} %bitcast.28), channel_id=1, source_target_pairs={{0,504},{4,508},{8,0},{12,4},{16,8},{20,12},{24,16},{28,20},{32,24... | collective-permute-start | bytes 786440 | tf_op jit(solution)/shard_map/ppermute | solution.py:15
  51.7 0.7 constant_dynamic-update-slice_fusion.6
  52.5 0.7 constant_dynamic-update-slice_fusion.5
  53.2 2.0 gather_fusion.1
  55.2 3.2 %reshape.61 = bf16[4,1024,4,64]{3,2,1,0:T(4,128)(2,1)} reshape(bf16[32,128,256]{2,1,0:T(8,128)(2,1)S(1)} %gather_fusion.1) | data formatting | bytes 4194304 | tf_op jit(solution)/shard_map/reshape | solution.py:52
  58.4 3.6 %fusion.4 = f32[4,4,128,1024]{3,2,1,0:T(8,128)S(1)} fusion(bf16[4,1024,4,64]{3,2,1,0:T(4,128)(2,1)} %reshape.61, bf16[4,128,4,64]{3,2,1,0:T(4,128)(2,1)} %reshape.60), kind=kOutput, calls=%fused_computation.7 | convolution fusion | flops 268435456 | bytes 10747904 | tf_op jit(solution)/shard_map/pqhd,pkhd->phqk/dot_general | solution.py:55
  62.1 2.2 %fusion.62 = f32[4,4,128]{2,1,0:T(4,128)S(1)} fusion(f32[4,4,128,1024]{3,2,1,0:T(8,128)S(1)} %fusion.4), kind=kOutput, calls=%fused_computation.87 | output fusion | flops 8389631 | bytes 8396800 | tf_op jit(solution)/shard_map/sub | solution.py:58
  64.2 1.0 copy-done.1
  65.3 1.7 constant_dynamic-update-slice_fusion.4
  67.0 1.7 constant_dynamic-update-slice_fusion.3
  68.6 0.7 constant_dynamic-update-slice_fusion.2
  69.4 1.7 constant_dynamic-update-slice_fusion.1
  71.1 1.7 constant_dynamic-update-slice_fusion
  72.7 2.0 gather_fusion
  74.7 3.3 %reshape.59 = bf16[4,1024,4,64]{3,2,1,0:T(4,128)(2,1)} reshape(bf16[32,128,256]{2,1,0:T(8,128)(2,1)S(1)} %gather_fusion) | data formatting | bytes 4194304 | tf_op jit(solution)/shard_map/reshape | solution.py:53
  78.0 12.1 %fusion.15 = bf16[4,128,4,64]{1,3,2,0:T(8,128)(2,1)S(1)} fusion(f32[4,4,128]{2,1,0:T(4,128)S(1)} %fusion.62, bf16[4,1024,4,64]{3,2,1,0:T(4,128)(2,1)} %reshape.59, f32[4,4,128,1024]{3,2,1,0:T(8,128)} %copy-done.1), kind=kOutput, calls=%fused_computation.24 | convolution fusion | flops 279055360 | bytes 10756096 | tf_op jit(solution)/shard_map/phqk,pkhd->pqhd/dot_general | solution.py:59
  90.2 0.2 copy.24
  90.4 1.4 convolution_convert_fusion
  91.8 0.0 reduce-scatter.3.cloned.1.call-update
  91.8 0.0 all-gather.2.cloned.1.call-start
  91.9 0.8 dynamic_slice.11
  92.7 28.3 %reduce-scatter.3.cloned.1.call-done = bf16[512,256]{1,0:T(8,128)(2,1)} async-done(((bf16[512,1024]{1,0:T(8,128)(2,1)}), bf16[512,256]{1,0:T(8,128)(2,1)}) %reduce-scatter.3.cloned.1.call-update) | async-done | bytes 262160 | tf_op jit(solution)/shard_map/reduce_scatter | solution.py:62
  121.1 1.1 multiply_reduce_fusion.1
  122.2 8.4 %psum.7 = f32[512]{0:T(512)S(1)} all-reduce(f32[512]{0:T(512)S(1)} %multiply_reduce_fusion.1), channel_id=1, replica_groups=mesh['patch'=128,'mp'=4] {'mp'}, use_global_device_ids=true, to_apply=%region_5.6 | all-reduce | flops 512 | bytes 4096 | tf_op jit(solution)/shard_map/psum | solution.py:71
  130.6 1.8 multiply_convert_fusion
  132.4 0.0 reduce-scatter.5.cloned.1.call-start
  132.4 32.9 %all-gather.2.cloned.1.call-done = bf16[512,1024]{1,0:T(8,128)(2,1)} async-done(((bf16[512,256]{1,0:T(8,128)(2,1)}), bf16[512,1024]{1,0:T(8,128)(2,1)}) %all-gather.2.cloned.1.call-update) | async-done | bytes 1048592 | tf_op jit(solution)/shard_map/all_gather | solution.py:74
  165.3 3.6 %convolution_convert_fusion.1 = bf16[512,1024]{1,0:T(8,128)(2,1)} fusion(bf16[512,1024]{1,0:T(8,128)(2,1)S(1)} %copy-done, bf16[512,1024]{1,0:T(8,128)(2,1)} %all-gather.2.cloned.1.call-done, bf16[1024,512]{1,0:T(8,128)(2,1)S(1)} %copy-done.7), kind=kOutput, calls=%fused_computation.19 | convolution fusion | flops 1076625408 | bytes 4194304 | tf_op jit(solution)/shard_map/dot_general | solution.py:78
  168.9 32.6 %reduce-scatter.5.cloned.1.call-done = bf16[512,256]{1,0:T(8,128)(2,1)} async-done(((bf16[512,1024]{1,0:T(8,128)(2,1)}), bf16[512,256]{1,0:T(8,128)(2,1)}) %reduce-scatter.5.cloned.1.call-update) | async-done | bytes 262160 | tf_op jit(solution)/shard_map/reduce_scatter | solution.py:79
  201.5 1.8 add_convert_fusion
  (31 shorter events, 0.1 us)
Async XLA Ops:
  6.5 158.8 %copy-start = (bf16[512,1024]{1,0:T(8,128)(2,1)S(1)}, bf16[512,1024]{1,0:T(8,128)(2,1)}, u32[]{:S(2)}) copy-start(bf16[512,1024]{1,0:T(8,128)(2,1)} %param.14) | copy-start | bytes 3145732
  6.5 23.1 %copy-start.2 = (bf16[512,1024]{1,0:T(8,128)(2,1)S(1)}, bf16[512,1024]{1,0:T(8,128)(2,1)}, u32[]{:S(2)}) copy-start(bf16[512,1024]{1,0:T(8,128)(2,1)} %param.8) | copy-start | bytes 3145732
  6.5 23.1 %copy-start.8 = (f32[1024]{0:T(1024)S(1)}, f32[1024]{0:T(1024)}, u32[]{:S(2)}) copy-start(f32[1024]{0:T(1024)} %param.9) | copy-start | bytes 12292
  6.5 114.5 %reduce-scatter.3.cloned.1.call-start = ((), (), s32[]{:S(2)}) async-start(), calls=%async_computation.2 | async-start | bytes 1310720 | tf_op jit(solution)/shard_map/reduce_scatter | solution.py:62
  6.5 23.1 %copy-start.6 = (bf16[3,1024,256]{2,1,0:T(8,128)(2,1)S(1)}, bf16[3,1024,256]{2,1,0:T(8,128)(2,1)}, u32[]{:S(2)}) copy-start(bf16[3,1024,256]{2,1,0:T(8,128)(2,1)} %param.10) | copy-start | bytes 4718596
  10.1 24.5 %collective-permute-start.4 = (bf16[4,128,256]{2,1,0:T(8,128)(2,1)S(1)}, bf16[4,128,256]{2,1,0:T(8,128)(2,1)}, u32[]{:S(2)}, u32[]{:S(2)}) collective-permute-start(bf16[4,128,256]{2,1,0:T(8,128)(2,1)S(1)} %bitcast.30), channel_id=1, source_target_pairs={{0,8},{4,12},{8,16},{12,20},{16,24},{20,28},{24,32},{28,36},{32,40... | collective-permute-start | bytes 786440 | tf_op jit(solution)/shard_map/ppermute | solution.py:15
  13.6 24.6 %collective-permute-start.5 = (bf16[4,128,256]{2,1,0:T(8,128)(2,1)S(1)}, bf16[4,128,256]{2,1,0:T(8,128)(2,1)}, u32[]{:S(2)}, u32[]{:S(2)}) collective-permute-start(bf16[4,128,256]{2,1,0:T(8,128)(2,1)S(1)} %bitcast.31), channel_id=1, source_target_pairs={{0,4},{4,8},{8,12},{12,16},{16,20},{20,24},{24,28},{28,32},{32,36}... | collective-permute-start | bytes 786440 | tf_op jit(solution)/shard_map/ppermute | solution.py:15
  15.5 28.7 %collective-permute-start.6 = (bf16[4,128,256]{2,1,0:T(8,128)(2,1)S(1)}, bf16[4,128,256]{2,1,0:T(8,128)(2,1)S(1)}, u32[]{:S(2)}, u32[]{:S(2)}) collective-permute-start(bf16[4,128,256]{2,1,0:T(8,128)(2,1)S(1)} %bitcast.32), channel_id=1, source_target_pairs={{0,508},{4,0},{8,4},{12,8},{16,12},{20,16},{24,20},{28,24},{32,28}... | collective-permute-start | bytes 786440 | tf_op jit(solution)/shard_map/ppermute | solution.py:15
  19.2 33.3 %collective-permute-start.7 = (bf16[4,128,256]{2,1,0:T(8,128)(2,1)S(1)}, bf16[4,128,256]{2,1,0:T(8,128)(2,1)S(1)}, u32[]{:S(2)}, u32[]{:S(2)}) collective-permute-start(bf16[4,128,256]{2,1,0:T(8,128)(2,1)S(1)} %bitcast.33), channel_id=1, source_target_pairs={{0,504},{4,508},{8,0},{12,4},{16,8},{20,12},{24,16},{28,20},{32,24... | collective-permute-start | bytes 786440 | tf_op jit(solution)/shard_map/ppermute | solution.py:15
  30.1 35.1 %collective-permute-start = (bf16[4,128,256]{2,1,0:T(8,128)(2,1)S(1)}, bf16[4,128,256]{2,1,0:T(8,128)(2,1)}, u32[]{:S(2)}, u32[]{:S(2)}) collective-permute-start(bf16[4,128,256]{2,1,0:T(8,128)(2,1)S(1)} %bitcast.25), channel_id=1, source_target_pairs={{0,8},{4,12},{8,16},{12,20},{16,24},{20,28},{24,32},{28,36},{32,40... | collective-permute-start | bytes 786440 | tf_op jit(solution)/shard_map/ppermute | solution.py:15
  34.6 32.4 %collective-permute-start.1 = (bf16[4,128,256]{2,1,0:T(8,128)(2,1)S(1)}, bf16[4,128,256]{2,1,0:T(8,128)(2,1)}, u32[]{:S(2)}, u32[]{:S(2)}) collective-permute-start(bf16[4,128,256]{2,1,0:T(8,128)(2,1)S(1)} %bitcast.26), channel_id=1, source_target_pairs={{0,4},{4,8},{8,12},{12,16},{16,20},{20,24},{24,28},{28,32},{32,36}... | collective-permute-start | bytes 786440 | tf_op jit(solution)/shard_map/ppermute | solution.py:15
  38.2 31.2 %collective-permute-start.2 = (bf16[4,128,256]{2,1,0:T(8,128)(2,1)S(1)}, bf16[4,128,256]{2,1,0:T(8,128)(2,1)}, u32[]{:S(2)}, u32[]{:S(2)}) collective-permute-start(bf16[4,128,256]{2,1,0:T(8,128)(2,1)S(1)} %bitcast.27), channel_id=1, source_target_pairs={{0,508},{4,0},{8,4},{12,8},{16,12},{20,16},{24,20},{28,24},{32,28}... | collective-permute-start | bytes 786440 | tf_op jit(solution)/shard_map/ppermute | solution.py:15
  44.2 26.9 %collective-permute-start.3 = (bf16[4,128,256]{2,1,0:T(8,128)(2,1)S(1)}, bf16[4,128,256]{2,1,0:T(8,128)(2,1)}, u32[]{:S(2)}, u32[]{:S(2)}) collective-permute-start(bf16[4,128,256]{2,1,0:T(8,128)(2,1)S(1)} %bitcast.28), channel_id=1, source_target_pairs={{0,504},{4,508},{8,0},{12,4},{16,8},{20,12},{24,16},{28,20},{32,24... | collective-permute-start | bytes 786440 | tf_op jit(solution)/shard_map/ppermute | solution.py:15
  62.0 3.2 %copy-start.1 = (f32[4,4,128,1024]{3,2,1,0:T(8,128)}, f32[4,4,128,1024]{3,2,1,0:T(8,128)S(1)}, u32[]{:S(2)}) copy-start(f32[4,4,128,1024]{3,2,1,0:T(8,128)S(1)} %fusion.4) | copy-start | bytes 25165828
  78.0 12.4 %copy-start.5 = (bf16[256,1024]{1,0:T(8,128)(2,1)S(1)}, bf16[256,1024]{1,0:T(8,128)(2,1)}, u32[]{:S(2)}) copy-start(bf16[256,1024]{1,0:T(8,128)(2,1)} %param.11) | copy-start | bytes 1572868
  90.1 30.9 %copy-start.3 = (bf16[512,1024]{1,0:T(8,128)(2,1)S(1)}, bf16[512,1024]{1,0:T(8,128)(2,1)}, u32[]{:S(2)}) copy-start(bf16[512,1024]{1,0:T(8,128)(2,1)} %param.8) | copy-start | bytes 3145732
  91.8 73.5 %copy-start.7 = (bf16[1024,512]{1,0:T(8,128)(2,1)S(1)}, bf16[1024,512]{1,0:T(8,128)(2,1)}, u32[]{:S(2)}) copy-start(bf16[1024,512]{1,0:T(8,128)(2,1)} %param.13) | copy-start | bytes 3145732
  91.8 73.5 %all-gather.2.cloned.1.call-start = ((), (), s32[]{:S(2)}) async-start(), calls=%async_computation.3 | async-start | bytes 1310720 | tf_op jit(solution)/shard_map/all_gather | solution.py:74
  132.4 69.1 %copy-start.4 = (bf16[512,256]{1,0:T(8,128)(2,1)S(1)}, bf16[512,256]{1,0:T(8,128)(2,1)}, u32[]{:S(2)}) copy-start(bf16[512,256]{1,0:T(8,128)(2,1)} %reduce-scatter.3.cloned.1.call-done) | copy-start | bytes 786436
  132.4 69.1 %reduce-scatter.5.cloned.1.call-start = ((), (), s32[]{:S(2)}) async-start(), calls=%async_computation.4 | async-start | bytes 1310720 | tf_op jit(solution)/shard_map/reduce_scatter | solution.py:79
Sparse Core Ops, SparseCore 0:
  92.0 29.0 reduce-scatter.2
  132.5 32.8 all-gather.1
  169.1 32.3 reduce-scatter.4
where the time goes:
time: 211 us; the launch traced here: 210 us
  waiting for transfers between devices  93.9 us (45%)
  starting transfers between devices  34.6 us (16%)
  local copies, waits for them, and re-layouts  26.8 us (13%)
  matrix products  23.6 us (11%)
  between operations  13.3 us (6%)
  other arithmetic  9.3 us (4%)
  blocking collectives  8.37 us (4%)
    ppermute x8, starting transfers between devices, from_behind(): lax.ppermute(array, axis, [(i, (i + by) % length) for i in range(length)])  34.5 us
    all_gather x1, waiting for transfers between devices, per_device(): normed2 = lax.all_gather(normed_cols, 'mp', axis=1, tiled=True)  32.9 us
    reduce_scatter x1, waiting for transfers between devices, per_device(): lax.psum_scatter(down_term.astype(jnp.bfloat16), 'mp', scatter_dimension=...  32.6 us
    reduce_scatter x1, waiting for transfers between devices, per_device(): lax.psum_scatter(partial_value.astype(jnp.bfloat16), 'mp', scatter_dimens...  28.3 us
    dot_general x1, matrix products, per_device(): jnp.einsum('phqk,pkhd->pqhd', probs, vals_nb, preferred_element_type=jnp....  12.1 us
    unnamed x26, local copies, waits for them, and re-layouts  11.6 us
    psum x1, blocking collectives, per_device(): square_sum = lax.psum(jnp.sum(residual_cols * residual_cols, axis=1), 'mp')  8.37 us
  transfers between devices with their start and end apart: 11, of which 3 were waited for; matrix products, arithmetic and copies ran while one was open for 12% of the time, Pallas kernels for 0%

commit v1 on v0

--- a/solution.py
+++ b/solution.py
@@ -71,7 +71,9 @@
     square_sum = lax.psum(jnp.sum(residual_cols * residual_cols, axis=1), "mp")
     inverse_rms = lax.rsqrt(square_sum / D + 1e-05)
     normed_cols = (residual_cols * inverse_rms[:, None] * gain_cols).astype(jnp.bfloat16)
-    normed2 = lax.all_gather(normed_cols, "mp", axis=1, tiled=True)
+    taken_in = jnp.stack([normed_cols] * lax.axis_size("mp"), axis=0)
+    value_now = lax.all_to_all(taken_in, axis_name="mp", split_axis=0, concat_axis=0)
+    normed2 = jnp.concatenate(value_now, 1)
     hidden = jax.nn.gelu(
         jnp.dot(normed2, w_up, preferred_element_type=jnp.float32), approximate=True
     ).astype(jnp.bfloat16)

time: 211 us -> 191 us (0.905)
  the two profiles are of different devices: /device:TPU:8 before, /device:TPU:16 now
where the time goes in v1:
time: 191 us; the launch traced here: 190 us
  waiting for transfers between devices  64.7 us (34%)
  starting transfers between devices  29.4 us (15%)
  local copies, waits for them, and re-layouts  27 us (14%)
  matrix products  23.7 us (12%)
  blocking collectives  22.8 us (12%)
  between operations  13.6 us (7%)
  other arithmetic  8.59 us (4%)
    reduce_scatter x1, waiting for transfers between devices, per_device(): lax.psum_scatter(partial_value.astype(jnp.bfloat16), 'mp', scatter_dimens...  33.5 us
    reduce_scatter x1, waiting for transfers between devices, per_device(): lax.psum_scatter(down_term.astype(jnp.bfloat16), 'mp', scatter_dimension=...  31.1 us
    ppermute x8, starting transfers between devices, from_behind(): lax.ppermute(array, axis, [(i, (i + by) % length) for i in range(length)])  29.3 us
    all_to_all x1, blocking collectives, per_device(): lax.all_to_all(taken_in, axis_name='mp', split_axis=0, concat_axis=0)  14.6 us
    dot_general x1, matrix products, per_device(): jnp.einsum('phqk,pkhd->pqhd', probs, vals_nb, preferred_element_type=jnp....  12.1 us
    unnamed x24, local copies, waits for them, and re-layouts  11.6 us
    psum x1, blocking collectives, per_device(): square_sum = lax.psum(jnp.sum(residual_cols * residual_cols, axis=1), 'mp')  8.24 us
  transfers between devices with their start and end apart: 10, of which 2 were waited for; matrix products, arithmetic and copies ran while one was open for 14% of the time, Pallas kernels for 0%

profile of v1, /device:TPU:16, one launch (start us, length us, event | category | flops | bytes accessed | tf_op | source)
XLA Modules:
  0.0 189.8 jit_solution(2145495423289908021)
XLA Ops:
  6.6 1.7 fusion.9
  8.2 1.9 convolution_convert_fusion.2
  10.1 3.2 %collective-permute-start.4 = (bf16[4,128,256]{2,1,0:T(8,128)(2,1)S(1)}, bf16[4,128,256]{2,1,0:T(8,128)(2,1)}, u32[]{:S(2)}, u32[]{:S(2)}) collective-permute-start(bf16[4,128,256]{2,1,0:T(8,128)(2,1)S(1)} %bitcast.34), channel_id=1, source_target_pairs={{0,8},{4,12},{8,16},{12,20},{16,24},{20,28},{24,32},{28,36},{32,40... | collective-permute-start | bytes 786440 | tf_op jit(solution)/shard_map/ppermute | solution.py:15
  13.3 1.9 %collective-permute-start.5 = (bf16[4,128,256]{2,1,0:T(8,128)(2,1)S(1)}, bf16[4,128,256]{2,1,0:T(8,128)(2,1)}, u32[]{:S(2)}, u32[]{:S(2)}) collective-permute-start(bf16[4,128,256]{2,1,0:T(8,128)(2,1)S(1)} %bitcast.35), channel_id=1, source_target_pairs={{0,4},{4,8},{8,12},{12,16},{16,20},{20,24},{24,28},{28,32},{32,36}... | collective-permute-start | bytes 786440 | tf_op jit(solution)/shard_map/ppermute | solution.py:15
  15.2 3.6 %collective-permute-start.6 = (bf16[4,128,256]{2,1,0:T(8,128)(2,1)S(1)}, bf16[4,128,256]{2,1,0:T(8,128)(2,1)S(1)}, u32[]{:S(2)}, u32[]{:S(2)}) collective-permute-start(bf16[4,128,256]{2,1,0:T(8,128)(2,1)S(1)} %bitcast.36), channel_id=1, source_target_pairs={{0,508},{4,0},{8,4},{12,8},{16,12},{20,16},{24,20},{28,24},{32,28}... | collective-permute-start | bytes 786440 | tf_op jit(solution)/shard_map/ppermute | solution.py:15
  18.9 2.7 %collective-permute-start.7 = (bf16[4,128,256]{2,1,0:T(8,128)(2,1)S(1)}, bf16[4,128,256]{2,1,0:T(8,128)(2,1)S(1)}, u32[]{:S(2)}, u32[]{:S(2)}) collective-permute-start(bf16[4,128,256]{2,1,0:T(8,128)(2,1)S(1)} %bitcast.37), channel_id=1, source_target_pairs={{0,504},{4,508},{8,0},{12,4},{16,8},{20,12},{24,16},{28,20},{32,24... | collective-permute-start | bytes 786440 | tf_op jit(solution)/shard_map/ppermute | solution.py:15
  21.6 0.5 convolution_convert_fusion.4
  22.1 3.2 %collective-permute-start = (bf16[4,128,256]{2,1,0:T(8,128)(2,1)S(1)}, bf16[4,128,256]{2,1,0:T(8,128)(2,1)}, u32[]{:S(2)}, u32[]{:S(2)}) collective-permute-start(bf16[4,128,256]{2,1,0:T(8,128)(2,1)S(1)} %bitcast.29), channel_id=1, source_target_pairs={{0,8},{4,12},{8,16},{12,20},{16,24},{20,28},{24,32},{28,36},{32,40... | collective-permute-start | bytes 786440 | tf_op jit(solution)/shard_map/ppermute | solution.py:15
  25.3 0.5 convolution_convert_fusion.3
  25.8 0.8 compare_select_fusion
  26.6 0.1 copy.18
  26.6 0.1 reshape.49
  26.7 1.0 reshape.70
  27.8 1.9 %collective-permute-start.1 = (bf16[4,128,256]{2,1,0:T(8,128)(2,1)S(1)}, bf16[4,128,256]{2,1,0:T(8,128)(2,1)}, u32[]{:S(2)}, u32[]{:S(2)}) collective-permute-start(bf16[4,128,256]{2,1,0:T(8,128)(2,1)S(1)} %bitcast.30), channel_id=1, source_target_pairs={{0,4},{4,8},{8,12},{12,16},{16,20},{20,24},{24,28},{28,32},{32,36}... | collective-permute-start | bytes 786440 | tf_op jit(solution)/shard_map/ppermute | solution.py:15
  29.7 1.7 constant_dynamic-update-slice_fusion.9
  31.4 3.6 %collective-permute-start.2 = (bf16[4,128,256]{2,1,0:T(8,128)(2,1)S(1)}, bf16[4,128,256]{2,1,0:T(8,128)(2,1)}, u32[]{:S(2)}, u32[]{:S(2)}) collective-permute-start(bf16[4,128,256]{2,1,0:T(8,128)(2,1)S(1)} %bitcast.31), channel_id=1, source_target_pairs={{0,508},{4,0},{8,4},{12,8},{16,12},{20,16},{24,20},{28,24},{32,28}... | collective-permute-start | bytes 786440 | tf_op jit(solution)/shard_map/ppermute | solution.py:15
  35.0 1.7 constant_dynamic-update-slice_fusion.8
  36.7 0.7 constant_dynamic-update-slice_fusion.7
  37.4 9.2 %collective-permute-start.3 = (bf16[4,128,256]{2,1,0:T(8,128)(2,1)S(1)}, bf16[4,128,256]{2,1,0:T(8,128)(2,1)}, u32[]{:S(2)}, u32[]{:S(2)}) collective-permute-start(bf16[4,128,256]{2,1,0:T(8,128)(2,1)S(1)} %bitcast.32), channel_id=1, source_target_pairs={{0,504},{4,508},{8,0},{12,4},{16,8},{20,12},{24,16},{28,20},{32,24... | collective-permute-start | bytes 786440 | tf_op jit(solution)/shard_map/ppermute | solution.py:15
  46.6 0.7 constant_dynamic-update-slice_fusion.6
  47.3 0.7 constant_dynamic-update-slice_fusion.5
  48.0 2.0 %gather_fusion.1 = bf16[32,128,256]{2,1,0:T(8,128)(2,1)S(1)} fusion(bf16[20,128,256]{2,1,0:T(8,128)(2,1)} %constant_dynamic-update-slice_fusion.5, s32[1024]{0:T(1024)S(1)} %pad_clamp_fusion), kind=kCustom, calls=%fused_computation.1 | custom fusion | bytes 4194432 | tf_op jit(solution)/shard_map/gather | solution.py:52
  50.0 3.3 %reshape.71 = bf16[4,1024,4,64]{3,2,1,0:T(4,128)(2,1)} reshape(bf16[32,128,256]{2,1,0:T(8,128)(2,1)S(1)} %gather_fusion.1) | data formatting | bytes 4194304 | tf_op jit(solution)/shard_map/reshape | solution.py:52
  53.3 3.6 %fusion.4 = f32[4,4,128,1024]{3,2,1,0:T(8,128)S(1)} fusion(bf16[4,1024,4,64]{3,2,1,0:T(4,128)(2,1)} %reshape.71, bf16[4,128,4,64]{3,2,1,0:T(4,128)(2,1)} %reshape.70), kind=kOutput, calls=%fused_computation.7 | convolution fusion | flops 268435456 | bytes 10747904 | tf_op jit(solution)/shard_map/pqhd,pkhd->phqk/dot_general | solution.py:55
  56.9 2.2 %fusion.62 = f32[4,4,128]{2,1,0:T(4,128)S(1)} fusion(f32[4,4,128,1024]{3,2,1,0:T(8,128)S(1)} %fusion.4), kind=kOutput, calls=%fused_computation.87 | output fusion | flops 8389631 | bytes 8396800 | tf_op jit(solution)/shard_map/sub | solution.py:58
  59.1 1.0 copy-done.1
  60.2 1.7 constant_dynamic-update-slice_fusion.4
  61.8 1.7 constant_dynamic-update-slice_fusion.3
  63.5 0.7 constant_dynamic-update-slice_fusion.2
  64.3 1.7 constant_dynamic-update-slice_fusion.1
  65.9 1.7 constant_dynamic-update-slice_fusion
  67.6 2.0 %gather_fusion = bf16[32,128,256]{2,1,0:T(8,128)(2,1)S(1)} fusion(bf16[20,128,256]{2,1,0:T(8,128)(2,1)} %constant_dynamic-update-slice_fusion, s32[1024]{0:T(1024)S(1)} %pad_clamp_fusion), kind=kCustom, calls=%fused_computation | custom fusion | bytes 4194432 | tf_op jit(solution)/shard_map/gather | solution.py:53
  69.6 3.3 %reshape.69 = bf16[4,1024,4,64]{3,2,1,0:T(4,128)(2,1)} reshape(bf16[32,128,256]{2,1,0:T(8,128)(2,1)S(1)} %gather_fusion) | data formatting | bytes 4194304 | tf_op jit(solution)/shard_map/reshape | solution.py:53
  72.9 12.1 %fusion.15 = bf16[4,128,4,64]{1,3,2,0:T(8,128)(2,1)S(1)} fusion(f32[4,4,128]{2,1,0:T(4,128)S(1)} %fusion.62, bf16[4,1024,4,64]{3,2,1,0:T(4,128)(2,1)} %reshape.69, f32[4,4,128,1024]{3,2,1,0:T(8,128)} %copy-done.1), kind=kOutput, calls=%fused_computation.24 | convolution fusion | flops 279055360 | bytes 10756096 | tf_op jit(solution)/shard_map/phqk,pkhd->pqhd/dot_general | solution.py:59
  85.1 0.2 copy.25
  85.3 1.5 convolution_convert_fusion
  86.8 0.0 reduce-scatter.5.cloned.1.call-start
  86.8 0.8 dynamic_slice.11
  87.6 33.5 %reduce-scatter.3.cloned.1.call-done = bf16[512,256]{1,0:T(8,128)(2,1)} async-done(((bf16[512,1024]{1,0:T(8,128)(2,1)}), bf16[512,256]{1,0:T(8,128)(2,1)}) %reduce-scatter.3.cloned.1.call-update) | async-done | bytes 262160 | tf_op jit(solution)/shard_map/reduce_scatter | solution.py:62
  121.1 1.1 multiply_reduce_fusion.1
  122.2 8.2 %psum.7 = f32[512]{0:T(512)S(1)} all-reduce(f32[512]{0:T(512)S(1)} %multiply_reduce_fusion.1), channel_id=1, replica_groups=mesh['patch'=128,'mp'=4] {'mp'}, use_global_device_ids=true, to_apply=%region_5.6 | all-reduce | flops 512 | bytes 4096 | tf_op jit(solution)/shard_map/psum | solution.py:71
  130.5 1.1 multiply_convert_fusion
  131.6 0.1 copy.26
  131.7 0.1 stack.2
  131.8 14.6 %all_to_all.5 = bf16[4,512,256]{1,2,0:T(8,128)(2,1)S(1)} all-to-all(bf16[4,512,256]{1,2,0:T(8,128)(2,1)S(1)} %stack.2), channel_id=1, replica_groups=mesh['patch'=128,'mp'=4] {'mp'}, dimensions={0} | all-to-all | bytes 2097152 | tf_op jit(solution)/shard_map/all_to_all | solution.py:75
  146.4 3.7 %convolution_convert_fusion.1 = bf16[512,1024]{1,0:T(8,128)(2,1)} fusion(bf16[512,1024]{1,0:T(8,128)(2,1)S(1)} %copy-done, bf16[512,1024]{0,1:T(8,128)(2,1)S(1)} %bitcast.28, bf16[1024,512]{1,0:T(8,128)(2,1)} %param.13), kind=kOutput, calls=%fused_computation.19 | convolution fusion | flops 1076625408 | bytes 4194304 | tf_op jit(solution)/shard_map/dot_general | solution.py:80
  150.1 31.1 %reduce-scatter.5.cloned.1.call-done = bf16[512,256]{1,0:T(8,128)(2,1)} async-done(((bf16[512,1024]{1,0:T(8,128)(2,1)}), bf16[512,256]{1,0:T(8,128)(2,1)}) %reduce-scatter.5.cloned.1.call-update) | async-done | bytes 262160 | tf_op jit(solution)/shard_map/reduce_scatter | solution.py:81
  181.2 1.8 add_convert_fusion
  (29 shorter events, 0.1 us)
Async XLA Ops:
  6.5 139.9 %copy-start = (bf16[512,1024]{1,0:T(8,128)(2,1)S(1)}, bf16[512,1024]{1,0:T(8,128)(2,1)}, u32[]{:S(2)}) copy-start(bf16[512,1024]{1,0:T(8,128)(2,1)} %param.14) | copy-start | bytes 3145732
  6.5 15.0 %copy-start.2 = (bf16[512,1024]{1,0:T(8,128)(2,1)S(1)}, bf16[512,1024]{1,0:T(8,128)(2,1)}, u32[]{:S(2)}) copy-start(bf16[512,1024]{1,0:T(8,128)(2,1)} %param.8) | copy-start | bytes 3145732
  6.5 15.0 %copy-start.7 = (f32[1024]{0:T(1024)S(1)}, f32[1024]{0:T(1024)}, u32[]{:S(2)}) copy-start(f32[1024]{0:T(1024)} %param.9) | copy-start | bytes 12292
  6.5 114.6 %reduce-scatter.3.cloned.1.call-start = ((), (), s32[]{:S(2)}) async-start(), calls=%async_computation.3 | async-start | bytes 1310720 | tf_op jit(solution)/shard_map/reduce_scatter | solution.py:62
  6.5 15.0 %copy-start.6 = (bf16[3,1024,256]{2,1,0:T(8,128)(2,1)S(1)}, bf16[3,1024,256]{2,1,0:T(8,128)(2,1)}, u32[]{:S(2)}) copy-start(bf16[3,1024,256]{2,1,0:T(8,128)(2,1)} %param.10) | copy-start | bytes 4718596
  10.1 17.7 %collective-permute-start.4 = (bf16[4,128,256]{2,1,0:T(8,128)(2,1)S(1)}, bf16[4,128,256]{2,1,0:T(8,128)(2,1)}, u32[]{:S(2)}, u32[]{:S(2)}) collective-permute-start(bf16[4,128,256]{2,1,0:T(8,128)(2,1)S(1)} %bitcast.34), channel_id=1, source_target_pairs={{0,8},{4,12},{8,16},{12,20},{16,24},{20,28},{24,32},{28,36},{32,40... | collective-permute-start | bytes 786440 | tf_op jit(solution)/shard_map/ppermute | solution.py:15
  13.3 18.1 %collective-permute-start.5 = (bf16[4,128,256]{2,1,0:T(8,128)(2,1)S(1)}, bf16[4,128,256]{2,1,0:T(8,128)(2,1)}, u32[]{:S(2)}, u32[]{:S(2)}) collective-permute-start(bf16[4,128,256]{2,1,0:T(8,128)(2,1)S(1)} %bitcast.35), channel_id=1, source_target_pairs={{0,4},{4,8},{8,12},{12,16},{16,20},{20,24},{24,28},{28,32},{32,36}... | collective-permute-start | bytes 786440 | tf_op jit(solution)/shard_map/ppermute | solution.py:15
  15.2 22.2 %collective-permute-start.6 = (bf16[4,128,256]{2,1,0:T(8,128)(2,1)S(1)}, bf16[4,128,256]{2,1,0:T(8,128)(2,1)S(1)}, u32[]{:S(2)}, u32[]{:S(2)}) collective-permute-start(bf16[4,128,256]{2,1,0:T(8,128)(2,1)S(1)} %bitcast.36), channel_id=1, source_target_pairs={{0,508},{4,0},{8,4},{12,8},{16,12},{20,16},{24,20},{28,24},{32,28}... | collective-permute-start | bytes 786440 | tf_op jit(solution)/shard_map/ppermute | solution.py:15
  18.9 28.4 %collective-permute-start.7 = (bf16[4,128,256]{2,1,0:T(8,128)(2,1)S(1)}, bf16[4,128,256]{2,1,0:T(8,128)(2,1)S(1)}, u32[]{:S(2)}, u32[]{:S(2)}) collective-permute-start(bf16[4,128,256]{2,1,0:T(8,128)(2,1)S(1)} %bitcast.37), channel_id=1, source_target_pairs={{0,504},{4,508},{8,0},{12,4},{16,8},{20,12},{24,16},{28,20},{32,24... | collective-permute-start | bytes 786440 | tf_op jit(solution)/shard_map/ppermute | solution.py:15
  22.1 38.1 %collective-permute-start = (bf16[4,128,256]{2,1,0:T(8,128)(2,1)S(1)}, bf16[4,128,256]{2,1,0:T(8,128)(2,1)}, u32[]{:S(2)}, u32[]{:S(2)}) collective-permute-start(bf16[4,128,256]{2,1,0:T(8,128)(2,1)S(1)} %bitcast.29), channel_id=1, source_target_pairs={{0,8},{4,12},{8,16},{12,20},{16,24},{20,28},{24,32},{28,36},{32,40... | collective-permute-start | bytes 786440 | tf_op jit(solution)/shard_map/ppermute | solution.py:15
  27.8 34.0 %collective-permute-start.1 = (bf16[4,128,256]{2,1,0:T(8,128)(2,1)S(1)}, bf16[4,128,256]{2,1,0:T(8,128)(2,1)}, u32[]{:S(2)}, u32[]{:S(2)}) collective-permute-start(bf16[4,128,256]{2,1,0:T(8,128)(2,1)S(1)} %bitcast.30), channel_id=1, source_target_pairs={{0,4},{4,8},{8,12},{12,16},{16,20},{20,24},{24,28},{28,32},{32,36}... | collective-permute-start | bytes 786440 | tf_op jit(solution)/shard_map/ppermute | solution.py:15
  31.4 32.9 %collective-permute-start.2 = (bf16[4,128,256]{2,1,0:T(8,128)(2,1)S(1)}, bf16[4,128,256]{2,1,0:T(8,128)(2,1)}, u32[]{:S(2)}, u32[]{:S(2)}) collective-permute-start(bf16[4,128,256]{2,1,0:T(8,128)(2,1)S(1)} %bitcast.31), channel_id=1, source_target_pairs={{0,508},{4,0},{8,4},{12,8},{16,12},{20,16},{24,20},{28,24},{32,28}... | collective-permute-start | bytes 786440 | tf_op jit(solution)/shard_map/ppermute | solution.py:15
  37.4 28.5 %collective-permute-start.3 = (bf16[4,128,256]{2,1,0:T(8,128)(2,1)S(1)}, bf16[4,128,256]{2,1,0:T(8,128)(2,1)}, u32[]{:S(2)}, u32[]{:S(2)}) collective-permute-start(bf16[4,128,256]{2,1,0:T(8,128)(2,1)S(1)} %bitcast.32), channel_id=1, source_target_pairs={{0,504},{4,508},{8,0},{12,4},{16,8},{20,12},{24,16},{28,20},{32,24... | collective-permute-start | bytes 786440 | tf_op jit(solution)/shard_map/ppermute | solution.py:15
  56.9 3.2 %copy-start.1 = (f32[4,4,128,1024]{3,2,1,0:T(8,128)}, f32[4,4,128,1024]{3,2,1,0:T(8,128)S(1)}, u32[]{:S(2)}) copy-start(f32[4,4,128,1024]{3,2,1,0:T(8,128)S(1)} %fusion.4) | copy-start | bytes 25165828
  72.9 12.4 %copy-start.5 = (bf16[256,1024]{1,0:T(8,128)(2,1)S(1)}, bf16[256,1024]{1,0:T(8,128)(2,1)}, u32[]{:S(2)}) copy-start(bf16[256,1024]{1,0:T(8,128)(2,1)} %param.11) | copy-start | bytes 1572868
  85.0 36.1 %copy-start.3 = (bf16[512,1024]{1,0:T(8,128)(2,1)S(1)}, bf16[512,1024]{1,0:T(8,128)(2,1)}, u32[]{:S(2)}) copy-start(bf16[512,1024]{1,0:T(8,128)(2,1)} %param.8) | copy-start | bytes 3145732
  86.8 94.5 %reduce-scatter.5.cloned.1.call-start = ((), (), s32[]{:S(2)}) async-start(), calls=%async_computation.4 | async-start | bytes 1310720 | tf_op jit(solution)/shard_map/reduce_scatter | solution.py:81
  146.4 34.8 %copy-start.4 = (bf16[512,256]{1,0:T(8,128)(2,1)S(1)}, bf16[512,256]{1,0:T(8,128)(2,1)}, u32[]{:S(2)}) copy-start(bf16[512,256]{1,0:T(8,128)(2,1)} %reduce-scatter.3.cloned.1.call-done) | copy-start | bytes 786436
Sparse Core Ops, SparseCore 0:
  86.9 34.1 reduce-scatter.2
  150.2 30.9 reduce-scatter.4
